TPU v7x, 512 devices: a whole 4x4x16 slice. The times are simulated.
512 devices in a mesh: grp: 16 (over x, y), clu: 32 (over z, core).
Axes of the slice: x: 4, y: 4, z: 16, core: 2. Of those that a mesh axis runs over, the one named last changes fastest.
Arguments:
- lower_inverse: bfloat16 [32, 2, 512, 512], P('clu', None, 'grp'), as said below
- upper_inverse: bfloat16 [32, 2, 512, 512], P('clu', None, 'grp'), as said below
- lower_factors: bfloat16 [32, 128, 2, 48, 512], P('clu', 'grp'), may hold values from -1.2578125 to 1.2578125
- upper_factors: bfloat16 [32, 128, 2, 48, 512], P('clu', 'grp'), may hold values from -1.2578125 to 1.2578125
- lower_ranks: int32 [32, 128], P('clu', 'grp'), may hold values from 16 to 48
- upper_ranks: int32 [32, 128], P('clu', 'grp'), may hold values from 16 to 48
- pivots: int32 [32, 512], P('clu'), may hold values from 0 to 511, each once within a row
- pair_lower: int32 [32, 512], P('clu', 'grp'), may hold values from 0 to 7
- pair_upper: int32 [32, 512], P('clu', 'grp'), may hold values from 0 to 7
- pair_owner: int32 [32, 512, 1], P('clu', 'grp'), may hold values from 0 to 31; in each aligned block of 32 rows (0 to 31, 32 to 63, ..., all dimensions but the last counted through in order) at most 2 rows name the same one
Outputs:
- lower_solved: bfloat16 [32, 128, 2, 48, 512], P('clu', 'grp')
- upper_solved: bfloat16 [32, 128, 2, 48, 512], P('clu', 'grp')
- arrived: bfloat16 [32, 16, 32, 2, 2, 2304], P('clu', 'grp')
Inputs may be any that keep to these rules, and one draw needn't show every extreme that they name: `lower_inverse`: each cluster's matrix is unit lower triangular: zeros above the diagonal, one on the real part's diagonal and zero on the imaginary part's. `upper_inverse`: each cluster's matrix is upper triangular: zeros below the diagonal in both parts. `pair_owner`: among the 32 pairs of one share, at most 2 name the same owner, and some share reaches it.
All inputs are finite; a program needn't handle non-finite values.
Results may differ from a plain program's by a relative error of at most 0.0058.
Values may be sent and summed in bfloat16 or wider, within the bound.
No kernel may reach another device: no remote copies, remote signals or barrier semaphores. Data moves between devices by JAX's collectives and lax.ppermute only.
A program may use at most 64 MiB of HBM per device.

v0:
```python
import jax
import jax.numpy as jnp
from jax import lax
from jax.sharding import PartitionSpec as P

SEND_CAP = 2


def mask_rows(factors, block_ranks):
    rank_width = factors.shape[2]
    row_index = lax.broadcasted_iota(jnp.int32, (factors.shape[0], rank_width), 1)
    row_mask = row_index < block_ranks[:, None]
    return jnp.where(row_mask[:, None, :, None], factors, jnp.zeros((), factors.dtype))


def product(left, right):
    return jnp.einsum("prb,psb->prs", left, right, preferred_element_type=jnp.float32)


def per_device(
    lower_inverse,
    upper_inverse,
    lower_factors,
    upper_factors,
    lower_ranks,
    upper_ranks,
    pivots,
    pair_lower,
    pair_upper,
    pair_owner,
):
    lower_masked = mask_rows(lower_factors[0], lower_ranks[0])
    upper_masked = mask_rows(upper_factors[0], upper_ranks[0])
    upper_pivoted = jnp.take(upper_masked, pivots[0], axis=3)
    block_count = lower_masked.shape[0]
    rank_width = lower_masked.shape[2]
    panel_count = lower_masked.shape[3]
    lower_real = lower_masked[:, 0].reshape(block_count * rank_width, panel_count)
    lower_imag = lower_masked[:, 1].reshape(block_count * rank_width, panel_count)
    upper_real = upper_pivoted[:, 0].reshape(block_count * rank_width, panel_count)
    upper_imag = upper_pivoted[:, 1].reshape(block_count * rank_width, panel_count)
    contract_last = (((1,), (1,)), ((), ()))
    lower_piece = lax.all_gather(lower_inverse, "grp", axis=2, tiled=True)
    upper_piece = lax.all_gather(upper_inverse, "grp", axis=2, tiled=True)
    piece_real = upper_piece[0, 0]
    piece_imag = upper_piece[0, 1]
    real_part = jnp.dot(lower_real, piece_real, preferred_element_type=jnp.float32) - jnp.dot(
        lower_imag, piece_imag, preferred_element_type=jnp.float32
    )
    imag_part = jnp.dot(lower_real, piece_imag, preferred_element_type=jnp.float32) + jnp.dot(
        lower_imag, piece_real, preferred_element_type=jnp.float32
    )
    lower_totals = jnp.stack([real_part, imag_part], 0)
    piece_real = lower_piece[0, 0]
    piece_imag = lower_piece[0, 1]
    real_part = lax.dot_general(
        upper_real, piece_real, contract_last, preferred_element_type=jnp.float32
    ) - lax.dot_general(upper_imag, piece_imag, contract_last, preferred_element_type=jnp.float32)
    imag_part = lax.dot_general(
        upper_real, piece_imag, contract_last, preferred_element_type=jnp.float32
    ) + lax.dot_general(upper_imag, piece_real, contract_last, preferred_element_type=jnp.float32)
    upper_totals = jnp.stack([real_part, imag_part], 0)
    lower_solved = jnp.transpose(
        lower_totals.astype(jnp.bfloat16).reshape(2, block_count, rank_width, panel_count),
        (1, 0, 2, 3),
    )
    upper_solved = jnp.transpose(
        upper_totals.astype(jnp.bfloat16).reshape(2, block_count, rank_width, panel_count),
        (1, 0, 2, 3),
    )
    left_blocks = lower_solved[pair_lower[0]]
    right_blocks = upper_solved[pair_upper[0]]
    pair_count = left_blocks.shape[0]
    real_part = product(left_blocks[:, 0], right_blocks[:, 0]) - product(
        left_blocks[:, 1], right_blocks[:, 1]
    )
    imag_part = product(left_blocks[:, 0], right_blocks[:, 1]) + product(
        left_blocks[:, 1], right_blocks[:, 0]
    )
    cores = (
        jnp.stack([real_part, imag_part], 1)
        .reshape(pair_count, 2 * rank_width * rank_width)
        .astype(jnp.bfloat16)
    )
    owners = pair_owner[0, :, 0]
    pair_ids = lax.broadcasted_iota(jnp.int32, (pair_count,), 0)
    same_owner = (owners[:, None] == owners[None, :]) & (pair_ids[None, :] < pair_ids[:, None])
    slots = jnp.sum(same_owner.astype(jnp.int32), axis=1)
    clusters = lax.axis_size("clu")
    target_slot = owners * SEND_CAP + slots
    slot_ids = lax.broadcasted_iota(jnp.int32, (clusters * SEND_CAP, pair_count), 0)
    one_hot = (slot_ids == target_slot[None, :]).astype(jnp.bfloat16)
    buffer = jnp.dot(one_hot, cores, preferred_element_type=jnp.float32).astype(jnp.bfloat16)
    buffer = buffer.reshape(clusters, SEND_CAP, 2, rank_width * rank_width)
    arrived = lax.all_to_all(buffer, "clu", split_axis=0, concat_axis=0, tiled=True)
    return (lower_solved[None], upper_solved[None], arrived[None, None])


def solution(mesh):
    in_specs = (
        P("clu", None, "grp", None),
        P("clu", None, "grp", None),
        P("clu", "grp", None, None, None),
        P("clu", "grp", None, None, None),
        P("clu", "grp"),
        P("clu", "grp"),
        P("clu", None),
        P("clu", "grp"),
        P("clu", "grp"),
        P("clu", "grp", None),
    )
    out_specs = (
        P("clu", "grp", None, None, None),
        P("clu", "grp", None, None, None),
        P("clu", "grp", None, None, None, None),
    )
    return jax.shard_map(
        per_device, mesh=mesh, in_specs=in_specs, out_specs=out_specs, check_vma=False
    )
```

profile of v0, /device:TPU:1, one launch (start us, length us, event | category | flops | bytes accessed | tf_op | source)
XLA Modules:
  0.0 210.7 jit_solution(4374763556248300210)
XLA Ops:
  7.2 0.7 all-gather.5.cloned.1.call-update
  8.0 0.7 all-gather.3.cloned.1.call-update
  8.7 2.6 %copy.48 = bf16[1,8,2,48,512]{3,1,4,2,0:T(8,128)(2,1)S(1)} copy(bf16[1,8,2,48,512]{4,3,2,1,0:T(8,128)(2,1)} %param.13) | data formatting | bytes 1572864 | tf_op args[3]
  11.4 2.5 %copy.43 = bf16[1,8,2,48,512]{3,1,4,2,0:T(8,128)(2,1)} copy(bf16[1,8,2,48,512]{4,3,2,1,0:T(8,128)(2,1)S(1)} %copy-done.8) | data formatting | bytes 1572864 | tf_op args[2]
  14.0 1.4 bitcast_select_fusion
  15.4 3.0 %gather_fusion = bf16[512,8,2,48]{3,1,2,0:T(8,128)(2,1)S(1)} fusion(bf16[8,2,48,512]{2,0,3,1:T(8,128)(2,1)} %bitcast_select_fusion, s32[1024]{0:T(1024)S(1)} %pad_clamp_fusion.2), kind=kCustom, calls=%fused_computation | custom fusion | bytes 1574912 | tf_op jit(solution)/shard_map/jit(_take)/gather | solution.py:34
  18.4 1.8 select_bitcast_fusion
  20.3 1.1 fusion.26
  21.4 2.6 %copy.49 = bf16[8,1,48,512]{3,2,0,1:T(8,128)(2,1)} copy(bf16[8,1,48,512]{2,0,1,3:T(8,128)(2,1)} %get-tuple-element.4) | data formatting | bytes 786432 | tf_op jit(solution)/shard_map/slice | solution.py:40
  24.0 0.7 copy.50
  24.8 1.1 fusion.27
  25.9 2.7 %copy.44 = bf16[8,1,48,512]{3,2,0,1:T(8,128)(2,1)} copy(bf16[8,1,48,512]{2,0,3,1:T(8,128)(2,1)} %get-tuple-element.6) | data formatting | bytes 786432 | tf_op jit(solution)/shard_map/slice | solution.py:38
  28.5 0.7 copy.45
  29.5 42.9 %all-gather.5.cloned.1.call-done = bf16[1,2,512,512]{3,2,1,0:T(8,128)(2,1)} async-done(((bf16[1,2,32,512]{3,2,1,0:T(8,128)(2,1)}), bf16[1,2,512,512]{3,2,1,0:T(8,128)(2,1)}) %all-gather.5.cloned.1.call-update) | async-done | bytes 1048592 | tf_op jit(solution)/shard_map/all_gather | solution.py:43
  72.4 2.3 %fusion.21 = f32[384,512]{1,0:T(8,128)} fusion(bf16[384,512]{1,0:T(8,128)(2,1)S(1)} %bitcast.132, bf16[1,2,512,512]{3,2,1,0:T(8,128)(2,1)} %all-gather.5.cloned.1.call-done), kind=kOutput, calls=%fused_computation.43 | convolution fusion | flops 201326592 | bytes 1703936 | tf_op jit(solution)/shard_map/dot_general | solution.py:59
  74.7 1.4 fusion.20
  76.2 56.5 %all-gather.3.cloned.1.call-done = bf16[1,2,512,512]{3,2,1,0:T(8,128)(2,1)} async-done(((bf16[1,2,32,512]{3,2,1,0:T(8,128)(2,1)}), bf16[1,2,512,512]{3,2,1,0:T(8,128)(2,1)}) %all-gather.3.cloned.1.call-update) | async-done | bytes 1048592 | tf_op jit(solution)/shard_map/all_gather | solution.py:44
  132.7 1.5 fusion.19
  134.2 1.4 fusion.18
  135.6 0.4 fusion.9
  136.0 0.4 fusion.8
  136.5 0.4 copy-done.2
  137.6 1.3 fusion.15
  138.9 2.4 %gather_fusion.1 = bf16[32,2,48,512]{3,2,1,0:T(8,128)(2,1)} fusion(bf16[8,2,48,512]{3,2,1,0:T(8,128)(2,1)S(1)} %get-tuple-element.12, s32[1024]{0:T(1024)S(1)} %pad_clamp_fusion.1), kind=kCustom, calls=%fused_computation.1 | custom fusion | bytes 6291584 | tf_op jit(solution)/shard_map/gather | solution.py:71
  141.3 2.4 %gather_fusion.2 = bf16[32,2,48,512]{3,2,1,0:T(8,128)(2,1)} fusion(bf16[8,2,48,512]{3,2,1,0:T(8,128)(2,1)S(1)} %get-tuple-element.7, s32[1024]{0:T(1024)S(1)} %pad_clamp_fusion), kind=kCustom, calls=%fused_computation.2 | custom fusion | bytes 6291584 | tf_op jit(solution)/shard_map/gather | solution.py:72
  143.8 2.6 %fusion = f32[32,48,48]{2,1,0:T(8,128)S(1)} fusion(bf16[32,2,48,512]{3,2,1,0:T(8,128)(2,1)} %gather_fusion.1, bf16[32,2,48,512]{3,2,1,0:T(8,128)(2,1)} %gather_fusion.2), kind=kOutput, calls=%fused_computation.11 | convolution fusion | flops 75497472 | bytes 3440640 | tf_op jit(solution)/shard_map/prb,psb->prs/dot_general | solution.py:17
  146.6 2.1 fusion.1
  149.0 0.6 fusion.13
  149.5 0.5 fusion.12
  150.3 1.4 convert_element_type.16
  152.2 50.9 %all_to_all.5 = bf16[32,2,2,2304]{3,2,1,0:T(2,128)(2,1)S(1)} all-to-all(bf16[32,2,2,2304]{3,2,1,0:T(2,128)(2,1)S(1)} %reshape.167), channel_id=1, replica_groups=mesh['grp'=16,'clu'=32] {'clu'}, dimensions={0} | all-to-all | bytes 1179648 | tf_op jit(solution)/shard_map/all_to_all | solution.py:95
  203.0 0.8 copy.63
  (49 shorter events, 2.6 us)
Async XLA Ops:
  7.2 4.1 %copy-start.10 = (s32[1,8]{1,0:T(1,128)S(1)}, s32[1,8]{1,0:T(1,128)}, u32[]{:S(2)}) copy-start(s32[1,8]{1,0:T(1,128)} %param.15) | copy-start | bytes 100
  7.2 4.2 %copy-start.9 = (s32[1,512]{1,0:T(1,128)S(1)}, s32[1,512]{1,0:T(1,128)}, u32[]{:S(2)}) copy-start(s32[1,512]{1,0:T(1,128)} %param.16) | copy-start | bytes 6148
  7.2 4.2 %copy-start.8 = (bf16[1,8,2,48,512]{4,3,2,1,0:T(8,128)(2,1)S(1)}, bf16[1,8,2,48,512]{4,3,2,1,0:T(8,128)(2,1)}, u32[]{:S(2)}) copy-start(bf16[1,8,2,48,512]{4,3,2,1,0:T(8,128)(2,1)} %param.12) | copy-start | bytes 2359300
  7.2 65.2 %all-gather.5.cloned.1.call-start = ((), (), s32[]{:S(2)}) async-start(), calls=%async_computation.2 | async-start | bytes 1114112 | tf_op jit(solution)/shard_map/all_gather | solution.py:43
  7.9 124.8 %all-gather.3.cloned.1.call-start = ((), (), s32[]{:S(2)}) async-start(), calls=%async_computation.1 | async-start | bytes 1114112 | tf_op jit(solution)/shard_map/all_gather | solution.py:44
  11.3 2.6 %copy-start.11 = (s32[1,8]{1,0:T(1,128)S(1)}, s32[1,8]{1,0:T(1,128)}, u32[]{:S(2)}) copy-start(s32[1,8]{1,0:T(1,128)} %param.14) | copy-start | bytes 100
  18.4 1.8 copy-start
  25.9 3.4 %copy-start.12 = (s32[1,32]{1,0:T(1,128)S(1)}, s32[1,32]{1,0:T(1,128)}, u32[]{:S(2)}) copy-start(s32[1,32]{1,0:T(1,128)} %param.17) | copy-start | bytes 388
  25.9 3.4 %copy-start.13 = (s32[1,32]{1,0:T(1,128)S(1)}, s32[1,32]{1,0:T(1,128)}, u32[]{:S(2)}) copy-start(s32[1,32]{1,0:T(1,128)} %param.18) | copy-start | bytes 388
  25.9 3.5 %copy-start.14 = (s32[1,32,1]{1,2,0:T(1,128)S(1)}, s32[1,32,1]{1,2,0:T(1,128)}, u32[]{:S(2)}) copy-start(s32[1,32,1]{1,2,0:T(1,128)} %param.19) | copy-start | bytes 388
  25.9 46.5 %copy-start.3 = (bf16[8,1,48,512]{3,2,0,1:T(8,128)(2,1)S(1)}, bf16[8,1,48,512]{3,2,0,1:T(8,128)(2,1)}, u32[]{:S(2)}) copy-start(bf16[8,1,48,512]{3,2,0,1:T(8,128)(2,1)} %copy.49) | copy-start | bytes 1179652
  29.3 103.4 %copy-start.4 = (bf16[8,1,48,512]{3,2,0,1:T(8,128)(2,1)S(1)}, bf16[8,1,48,512]{3,2,0,1:T(8,128)(2,1)}, u32[]{:S(2)}) copy-start(bf16[8,1,48,512]{3,2,0,1:T(8,128)(2,1)} %copy.44) | copy-start | bytes 1179652
  76.2 59.4 %copy-start.1 = (bf16[1,2,512,512]{3,2,1,0:T(8,128)(2,1)S(1)}, bf16[1,2,512,512]{3,2,1,0:T(8,128)(2,1)}, u32[]{:S(2)}) copy-start(bf16[1,2,512,512]{3,2,1,0:T(8,128)(2,1)} %all-gather.5.cloned.1.call-done) | copy-start | bytes 3145732
  132.7 2.9 %copy-start.7 = (f32[384,512]{1,0:T(8,128)S(1)}, f32[384,512]{1,0:T(8,128)}, u32[]{:S(2)}) copy-start(f32[384,512]{1,0:T(8,128)} %fusion.21) | copy-start | bytes 2359300
  135.6 1.2 copy-start.2
  143.8 2.8 %copy-start.5 = (bf16[32,2,48,512]{3,2,1,0:T(8,128)(2,1)S(1)}, bf16[32,2,48,512]{3,2,1,0:T(8,128)(2,1)}, u32[]{:S(2)}) copy-start(bf16[32,2,48,512]{3,2,1,0:T(8,128)(2,1)} %gather_fusion.1) | copy-start | bytes 9437188
  146.6 2.4 %copy-start.6 = (bf16[32,2,48,512]{3,2,1,0:T(8,128)(2,1)S(1)}, bf16[32,2,48,512]{3,2,1,0:T(8,128)(2,1)}, u32[]{:S(2)}) copy-start(bf16[32,2,48,512]{3,2,1,0:T(8,128)(2,1)} %gather_fusion.2) | copy-start | bytes 9437188
Sparse Core Ops, SparseCore 0:
  11.1 61.2 all-gather.4
  75.5 57.1 all-gather.2
where the time goes:
time: 211 us
  waiting for transfers between devices  101 us (48%)
  blocking collectives  50.9 us (24%)
  local copies, waits for them, and re-layouts  25.2 us (12%)
  between operations  14.4 us (7%)
  matrix products  14.2 us (7%)
  other arithmetic  5.23 us (2%)
    all_gather x1, waiting for transfers between devices, per_device(): upper_piece = lax.all_gather(upper_inverse, 'grp', axis=2, tiled=True)  56.5 us
    all_to_all x1, blocking collectives, per_device(): lax.all_to_all(buffer, 'clu', split_axis=0, concat_axis=0, tiled=True)  50.9 us
    all_gather x1, waiting for transfers between devices, per_device(): lower_piece = lax.all_gather(lower_inverse, 'grp', axis=2, tiled=True)  42.9 us
    unnamed x33, local copies, waits for them, and re-layouts  6.88 us
    dot_general x4, matrix products, product(): jnp.einsum('prb,psb->prs', left, right, preferred_element_type=jnp.float32)  5.78 us
  transfers between devices with their start and end apart: 2, of which 2 were waited for; matrix products, arithmetic and copies ran while one was open for 12% of the time, Pallas kernels for 0%

commit v1 on v0

--- a/solution.py
+++ b/solution.py
@@ -4,6 +4,12 @@
 from jax.sharding import PartitionSpec as P
 
 SEND_CAP = 2
+
+
+def laid_out(blocks, dim):
+    blocks = jnp.moveaxis(blocks, 0, dim)
+    shape = blocks.shape
+    return blocks.reshape(*shape[:dim], shape[dim] * shape[dim + 1], *shape[dim + 2 :])
 
 
 def mask_rows(factors, block_ranks):
@@ -41,7 +47,19 @@
     upper_imag = upper_pivoted[:, 1].reshape(block_count * rank_width, panel_count)
     contract_last = (((1,), (1,)), ((), ()))
     lower_piece = lax.all_gather(lower_inverse, "grp", axis=2, tiled=True)
-    upper_piece = lax.all_gather(upper_inverse, "grp", axis=2, tiled=True)
+    count = lax.axis_size("grp")
+    pairs = [(i, (i + 1) % count) for i in range(count)]
+    back = [(b, a) for a, b in pairs]
+    lower, upper = ([], [])
+    for hop in range(count - 1):
+        if hop % 2 == 0:
+            lower.append(lax.ppermute(lower[-1] if lower else upper_inverse, "grp", pairs))
+        else:
+            upper.append(lax.ppermute(upper[-1] if upper else upper_inverse, "grp", back))
+    blocks = jnp.stack([*lower[::-1], upper_inverse, *upper])
+    shift = lax.axis_index("grp") - len(lower)
+    blocks = blocks[(jnp.arange(count) - shift) % count]
+    upper_piece = laid_out(blocks, 2)
     piece_real = upper_piece[0, 0]
     piece_imag = upper_piece[0, 1]
     real_part = jnp.dot(lower_real, piece_real, preferred_element_type=jnp.float32) - jnp.dot(

time: 211 us -> 199 us (0.943)
  waiting for transfers between devices: 101 us -> 6.34 us
  starting transfers between devices: 0.08 us -> 63.3 us
  local copies, waits for them, and re-layouts: 25.2 us -> 37.8 us
  blocking collectives: 50.9 us -> 58.4 us
  matrix products: 14.2 us -> 11.3 us
    ppermute x0 -> x15, starting transfers between devices: none -> 63.3 us  [the longest x7 45.8 us: per_device(): lax.ppermute(upper[-1] if upper else upper_inverse, 'grp', back)]
    all_gather x1 -> x0, waiting for transfers between devices: 56.5 us -> none  [per_device(): upper_piece = lax.all_gather(upper_inverse, 'grp', axis=2, tiled=True)]
    all_gather x1, waiting for transfers between devices: 42.9 us -> 0.02 us  [per_device(): lower_piece = lax.all_gather(lower_inverse, 'grp', axis=2, tiled=True)]
    unnamed x33 -> x62, local copies, waits for them, and re-layouts: 6.88 us -> 20 us
    all_to_all x1, blocking collectives: 50.9 us -> 58.4 us  [per_device(): lax.all_to_all(buffer, 'clu', split_axis=0, concat_axis=0, tiled=True)]
    ppermute x0 -> x15, waiting for transfers between devices: none -> 6.3 us  [the longest x8 6.28 us: per_device(): lax.ppermute(lower[-1] if lower else upper_inverse, 'grp', pairs)]
  transfers between devices with their start and end apart: 2 -> 16, of which waited for: 2 -> 2; matrix products, arithmetic and copies ran while one was open for 12% -> 18% of each run, Pallas kernels for 0% -> 0%
where the time goes in v1:
time: 199 us; the launch traced here: 198 us
  starting transfers between devices  63.3 us (32%)
  blocking collectives  58.4 us (29%)
  local copies, waits for them, and re-layouts  37.8 us (19%)
  between operations  14.7 us (7%)
  matrix products  11.3 us (6%)
  waiting for transfers between devices  6.34 us (3%)
  other arithmetic  5.89 us (3%)
    all_to_all x1, blocking collectives, per_device(): lax.all_to_all(buffer, 'clu', split_axis=0, concat_axis=0, tiled=True)  58.4 us
    ppermute x7, starting transfers between devices, per_device(): lax.ppermute(upper[-1] if upper else upper_inverse, 'grp', back)  45.8 us
    unnamed x62, local copies, waits for them, and re-layouts  20 us
    ppermute x8, starting transfers between devices, per_device(): lax.ppermute(lower[-1] if lower else upper_inverse, 'grp', pairs)  17.4 us
    ppermute x8, waiting for transfers between devices, per_device(): lax.ppermute(lower[-1] if lower else upper_inverse, 'grp', pairs)  6.28 us
    dot_general x4, matrix products, product(): jnp.einsum('prb,psb->prs', left, right, preferred_element_type=jnp.float32)  5.77 us
  transfers between devices with their start and end apart: 16, of which 2 were waited for; matrix products, arithmetic and copies ran while one was open for 18% of the time, Pallas kernels for 0%

profile of v1, /device:TPU:1, one launch (start us, length us, event | category | flops | bytes accessed | tf_op | source)
XLA Modules:
  0.0 197.7 jit_solution(2051371274657716711)
XLA Ops:
  7.2 4.0 %collective-permute-start = (bf16[1,2,32,512]{3,2,1,0:T(8,128)(2,1)}, bf16[1,2,32,512]{3,2,1,0:T(8,128)(2,1)S(1)}, u32[]{:S(2)}, u32[]{:S(2)}) collective-permute-start(bf16[1,2,32,512]{3,2,1,0:T(8,128)(2,1)} %param.11), channel_id=1, source_target_pairs={{0,32},{32,64},{64,96},{96,128},{128,160},{160,192},{192,224},{224... | collective-permute-start | bytes 196616 | tf_op jit(solution)/shard_map/ppermute | solution.py:56
  11.3 5.6 %collective-permute-start.8 = (bf16[1,2,32,512]{3,2,1,0:T(8,128)(2,1)}, bf16[1,2,32,512]{3,2,1,0:T(8,128)(2,1)S(1)}, u32[]{:S(2)}, u32[]{:S(2)}) collective-permute-start(bf16[1,2,32,512]{3,2,1,0:T(8,128)(2,1)} %param.11), channel_id=1, source_target_pairs={{32,0},{64,32},{96,64},{128,96},{160,128},{192,160},{224,192},{256... | collective-permute-start | bytes 196616 | tf_op jit(solution)/shard_map/ppermute | solution.py:58
  16.9 2.6 %copy.76 = bf16[1,8,2,48,512]{3,1,4,2,0:T(8,128)(2,1)S(1)} copy(bf16[1,8,2,48,512]{4,3,2,1,0:T(8,128)(2,1)} %param.13) | data formatting | bytes 1572864 | tf_op args[3]
  19.6 1.5 bitcast_select_fusion
  21.1 3.0 %gather_fusion.1 = bf16[512,8,2,48]{3,1,2,0:T(8,128)(2,1)S(1)} fusion(bf16[8,2,48,512]{2,0,3,1:T(8,128)(2,1)} %bitcast_select_fusion, s32[1024]{0:T(1024)S(1)} %pad_clamp_fusion.2), kind=kCustom, calls=%fused_computation.1 | custom fusion | bytes 1574912 | tf_op jit(solution)/shard_map/jit(_take)/gather | solution.py:40
  24.0 1.8 select_bitcast_fusion
  26.9 2.6 %copy.57 = bf16[1,8,2,48,512]{3,1,4,2,0:T(8,128)(2,1)S(1)} copy(bf16[1,8,2,48,512]{4,3,2,1,0:T(8,128)(2,1)} %param.12) | data formatting | bytes 1572864 | tf_op args[2]
  30.9 1.9 collective-permute-start.1
  33.0 6.2 %collective-permute-done.1 = bf16[1,2,32,512]{3,2,1,0:T(8,128)(2,1)S(1)} collective-permute-done((bf16[1,2,32,512]{3,2,1,0:T(8,128)(2,1)S(1)}, bf16[1,2,32,512]{3,2,1,0:T(8,128)(2,1)S(1)}, u32[]{:S(2)}, u32[]{:S(2)}) %collective-permute-start.1) | collective-permute-done | bytes 65568 | tf_op jit(solution)/shard_map/ppermute | solution.py:56
  39.2 1.9 collective-permute-start.2
  41.2 6.7 %collective-permute-start.9 = (bf16[1,2,32,512]{3,2,1,0:T(8,128)(2,1)S(1)}, bf16[1,2,32,512]{3,2,1,0:T(8,128)(2,1)}, u32[]{:S(2)}, u32[]{:S(2)}) collective-permute-start(bf16[1,2,32,512]{3,2,1,0:T(8,128)(2,1)S(1)} %collective-permute-done.8), channel_id=1, source_target_pairs={{32,0},{64,32},{96,64},{128,96},{160,128},{192,160},{224,192},{256... | collective-permute-start | bytes 196616 | tf_op jit(solution)/shard_map/ppermute | solution.py:58
  47.9 1.9 collective-permute-start.3
  49.9 6.7 %collective-permute-start.10 = (bf16[1,2,32,512]{3,2,1,0:T(8,128)(2,1)}, bf16[1,2,32,512]{3,2,1,0:T(8,128)(2,1)}, u32[]{:S(2)}, u32[]{:S(2)}) collective-permute-start(bf16[1,2,32,512]{3,2,1,0:T(8,128)(2,1)} %collective-permute-done.9), channel_id=1, source_target_pairs={{32,0},{64,32},{96,64},{128,96},{160,128},{192,160},{224,192},{256... | collective-permute-start | bytes 196616 | tf_op jit(solution)/shard_map/ppermute | solution.py:58
  56.6 1.9 collective-permute-start.4
  59.1 1.5 copy.77
  63.3 6.7 %collective-permute-start.11 = (bf16[1,2,32,512]{3,2,1,0:T(8,128)(2,1)}, bf16[1,2,32,512]{3,2,1,0:T(8,128)(2,1)S(1)}, u32[]{:S(2)}, u32[]{:S(2)}) collective-permute-start(bf16[1,2,32,512]{3,2,1,0:T(8,128)(2,1)} %collective-permute-done.10), channel_id=1, source_target_pairs={{32,0},{64,32},{96,64},{128,96},{160,128},{192,160},{224,192},{256... | collective-permute-start | bytes 196616 | tf_op jit(solution)/shard_map/ppermute | solution.py:58
  70.0 1.9 collective-permute-start.5
  72.0 6.7 %collective-permute-start.12 = (bf16[1,2,32,512]{3,2,1,0:T(8,128)(2,1)S(1)}, bf16[1,2,32,512]{3,2,1,0:T(8,128)(2,1)S(1)}, u32[]{:S(2)}, u32[]{:S(2)}) collective-permute-start(bf16[1,2,32,512]{3,2,1,0:T(8,128)(2,1)S(1)} %collective-permute-done.11), channel_id=1, source_target_pairs={{32,0},{64,32},{96,64},{128,96},{160,128},{192,160},{224,192},{256... | collective-permute-start | bytes 196616 | tf_op jit(solution)/shard_map/ppermute | solution.py:58
  78.7 1.9 collective-permute-start.6
  80.6 6.7 %collective-permute-start.13 = (bf16[1,2,32,512]{3,2,1,0:T(8,128)(2,1)S(1)}, bf16[1,2,32,512]{3,2,1,0:T(8,128)(2,1)S(1)}, u32[]{:S(2)}, u32[]{:S(2)}) collective-permute-start(bf16[1,2,32,512]{3,2,1,0:T(8,128)(2,1)S(1)} %collective-permute-done.12), channel_id=1, source_target_pairs={{32,0},{64,32},{96,64},{128,96},{160,128},{192,160},{224,192},{256... | collective-permute-start | bytes 196616 | tf_op jit(solution)/shard_map/ppermute | solution.py:58
  87.3 1.9 collective-permute-start.7
  89.3 6.9 %collective-permute-start.14 = (bf16[1,2,32,512]{3,2,1,0:T(8,128)(2,1)S(1)}, bf16[1,2,32,512]{3,2,1,0:T(8,128)(2,1)S(1)}, u32[]{:S(2)}, u32[]{:S(2)}) collective-permute-start(bf16[1,2,32,512]{3,2,1,0:T(8,128)(2,1)S(1)} %collective-permute-done.13), channel_id=1, source_target_pairs={{32,0},{64,32},{96,64},{128,96},{160,128},{192,160},{224,192},{256... | collective-permute-start | bytes 196616 | tf_op jit(solution)/shard_map/ppermute | solution.py:58
  98.0 1.5 bitcast_dynamic-update-slice_fusion.9
  99.5 1.5 bitcast_dynamic-update-slice_fusion.8
  105.6 1.5 bitcast_dynamic-update-slice_fusion.3
  109.5 1.8 gather_fusion
  113.2 1.5 fusion.21
  118.4 2.4 %gather_fusion.2 = bf16[32,2,48,512]{3,2,1,0:T(8,128)(2,1)} fusion(bf16[8,2,48,512]{3,2,1,0:T(8,128)(2,1)S(1)} %get-tuple-element.14, s32[1024]{0:T(1024)S(1)} %get-tuple-element.12), kind=kCustom, calls=%fused_computation.2 | custom fusion | bytes 6291584 | tf_op jit(solution)/shard_map/gather | solution.py:89
  120.8 2.4 %gather_fusion.3 = bf16[32,2,48,512]{3,2,1,0:T(8,128)(2,1)} fusion(bf16[8,2,48,512]{3,2,1,0:T(8,128)(2,1)S(1)} %get-tuple-element.7, s32[1024]{0:T(1024)S(1)} %get-tuple-element.11), kind=kCustom, calls=%fused_computation.3 | custom fusion | bytes 6291584 | tf_op jit(solution)/shard_map/gather | solution.py:90
  123.2 2.6 %fusion = f32[32,48,48]{2,1,0:T(8,128)S(1)} fusion(bf16[32,2,48,512]{3,2,1,0:T(8,128)(2,1)} %gather_fusion.2, bf16[32,2,48,512]{3,2,1,0:T(8,128)(2,1)} %gather_fusion.3), kind=kOutput, calls=%fused_computation.12 | convolution fusion | flops 75497472 | bytes 3440640 | tf_op jit(solution)/shard_map/prb,psb->prs/dot_general | solution.py:23
  126.0 2.1 %fusion.1 = f32[32,48,48]{2,1,0:T(8,128)S(1)} fusion(bf16[32,2,48,512]{3,2,1,0:T(8,128)(2,1)S(1)} %copy-done.4, bf16[32,2,48,512]{3,2,1,0:T(8,128)(2,1)} %gather_fusion.3), kind=kOutput, calls=%fused_computation.13 | convolution fusion | flops 75497472 | bytes 3440640 | tf_op jit(solution)/shard_map/prb,psb->prs/dot_general | solution.py:23
  131.6 58.4 %all_to_all.5 = bf16[32,2,2,2304]{3,2,1,0:T(2,128)(2,1)S(1)} all-to-all(bf16[32,2,2,2304]{3,2,1,0:T(2,128)(2,1)S(1)} %reshape.220), channel_id=1, replica_groups=mesh['grp'=16,'clu'=32] {'clu'}, dimensions={0} | all-to-all | bytes 1179648 | tf_op jit(solution)/shard_map/all_to_all | solution.py:113
  (109 shorter events, 25.0 us)
Async XLA Ops:
  7.2 12.3 %copy-start.17 = (s32[1,8]{1,0:T(1,128)S(1)}, s32[1,8]{1,0:T(1,128)}, u32[]{:S(2)}) copy-start(s32[1,8]{1,0:T(1,128)} %param.15) | copy-start | bytes 100
  7.2 12.4 %copy-start.15 = (s32[1,512]{1,0:T(1,128)S(1)}, s32[1,512]{1,0:T(1,128)}, u32[]{:S(2)}) copy-start(s32[1,512]{1,0:T(1,128)} %param.16) | copy-start | bytes 6148
  7.2 105.8 %all-gather.2.cloned.1.call-start = ((), (), s32[]{:S(2)}) async-start(), calls=%async_computation.1 | async-start | bytes 1114112 | tf_op jit(solution)/shard_map/all_gather | solution.py:49
  7.2 23.7 %collective-permute-start = (bf16[1,2,32,512]{3,2,1,0:T(8,128)(2,1)}, bf16[1,2,32,512]{3,2,1,0:T(8,128)(2,1)S(1)}, u32[]{:S(2)}, u32[]{:S(2)}) collective-permute-start(bf16[1,2,32,512]{3,2,1,0:T(8,128)(2,1)} %param.11), channel_id=1, source_target_pairs={{0,32},{32,64},{64,96},{96,128},{128,160},{160,192},{192,224},{224... | collective-permute-start | bytes 196616 | tf_op jit(solution)/shard_map/ppermute | solution.py:56
  11.3 29.9 %collective-permute-start.8 = (bf16[1,2,32,512]{3,2,1,0:T(8,128)(2,1)}, bf16[1,2,32,512]{3,2,1,0:T(8,128)(2,1)S(1)}, u32[]{:S(2)}, u32[]{:S(2)}) collective-permute-start(bf16[1,2,32,512]{3,2,1,0:T(8,128)(2,1)} %param.11), channel_id=1, source_target_pairs={{32,0},{64,32},{96,64},{128,96},{160,128},{192,160},{224,192},{256... | collective-permute-start | bytes 196616 | tf_op jit(solution)/shard_map/ppermute | solution.py:58
  29.8 20.1 %copy-start.20 = (s32[1,32]{1,0:T(1,128)S(1)}, s32[1,32]{1,0:T(1,128)}, u32[]{:S(2)}) copy-start(s32[1,32]{1,0:T(1,128)} %param.18) | copy-start | bytes 388
  29.8 28.8 %copy-start.21 = (s32[1,32]{1,0:T(1,128)S(1)}, s32[1,32]{1,0:T(1,128)}, u32[]{:S(2)}) copy-start(s32[1,32]{1,0:T(1,128)} %param.17) | copy-start | bytes 388
  29.8 29.4 %copy-start.1 = (bf16[8,1,48,512]{2,0,1,3:T(8,128)(2,1)S(1)}, bf16[8,1,48,512]{2,0,1,3:T(8,128)(2,1)}, u32[]{:S(2)}) copy-start(bf16[8,1,48,512]{2,0,1,3:T(8,128)(2,1)} %get-tuple-element.4) | copy-start | bytes 1179652
  30.9 29.7 %copy-start.9 = (bf16[1,2,32,512]{3,2,1,0:T(8,128)(2,1)}, bf16[1,2,32,512]{3,2,1,0:T(8,128)(2,1)S(1)}, u32[]{:S(2)}) copy-start(bf16[1,2,32,512]{3,2,1,0:T(8,128)(2,1)S(1)} %collective-permute-done) | copy-start | bytes 196612
  30.9 8.3 %collective-permute-start.1 = (bf16[1,2,32,512]{3,2,1,0:T(8,128)(2,1)S(1)}, bf16[1,2,32,512]{3,2,1,0:T(8,128)(2,1)S(1)}, u32[]{:S(2)}, u32[]{:S(2)}) collective-permute-start(bf16[1,2,32,512]{3,2,1,0:T(8,128)(2,1)S(1)} %collective-permute-done), channel_id=1, source_target_pairs={{0,32},{32,64},{64,96},{96,128},{128,160},{160,192},{192,224},{224... | collective-permute-start | bytes 196616 | tf_op jit(solution)/shard_map/ppermute | solution.py:56
  39.2 10.6 %copy-start.11 = (bf16[1,2,32,512]{3,2,1,0:T(8,128)(2,1)}, bf16[1,2,32,512]{3,2,1,0:T(8,128)(2,1)S(1)}, u32[]{:S(2)}) copy-start(bf16[1,2,32,512]{3,2,1,0:T(8,128)(2,1)S(1)} %collective-permute-done.1) | copy-start | bytes 196612
  39.2 8.6 %collective-permute-start.2 = (bf16[1,2,32,512]{3,2,1,0:T(8,128)(2,1)S(1)}, bf16[1,2,32,512]{3,2,1,0:T(8,128)(2,1)S(1)}, u32[]{:S(2)}, u32[]{:S(2)}) collective-permute-start(bf16[1,2,32,512]{3,2,1,0:T(8,128)(2,1)S(1)} %collective-permute-done.1), channel_id=1, source_target_pairs={{0,32},{32,64},{64,96},{96,128},{128,160},{160,192},{192,224},{224... | collective-permute-start | bytes 196616 | tf_op jit(solution)/shard_map/ppermute | solution.py:56
  41.2 19.4 %copy-start.7 = (bf16[1,2,32,512]{3,2,1,0:T(8,128)(2,1)}, bf16[1,2,32,512]{3,2,1,0:T(8,128)(2,1)S(1)}, u32[]{:S(2)}) copy-start(bf16[1,2,32,512]{3,2,1,0:T(8,128)(2,1)S(1)} %collective-permute-done.8) | copy-start | bytes 196612
  41.2 8.7 %collective-permute-start.9 = (bf16[1,2,32,512]{3,2,1,0:T(8,128)(2,1)S(1)}, bf16[1,2,32,512]{3,2,1,0:T(8,128)(2,1)}, u32[]{:S(2)}, u32[]{:S(2)}) collective-permute-start(bf16[1,2,32,512]{3,2,1,0:T(8,128)(2,1)S(1)} %collective-permute-done.8), channel_id=1, source_target_pairs={{32,0},{64,32},{96,64},{128,96},{160,128},{192,160},{224,192},{256... | collective-permute-start | bytes 196616 | tf_op jit(solution)/shard_map/ppermute | solution.py:58
  47.9 8.7 %copy-start.13 = (bf16[1,2,32,512]{3,2,1,0:T(8,128)(2,1)}, bf16[1,2,32,512]{3,2,1,0:T(8,128)(2,1)S(1)}, u32[]{:S(2)}) copy-start(bf16[1,2,32,512]{3,2,1,0:T(8,128)(2,1)S(1)} %collective-permute-done.2) | copy-start | bytes 196612
  47.9 8.7 %collective-permute-start.3 = (bf16[1,2,32,512]{3,2,1,0:T(8,128)(2,1)S(1)}, bf16[1,2,32,512]{3,2,1,0:T(8,128)(2,1)}, u32[]{:S(2)}, u32[]{:S(2)}) collective-permute-start(bf16[1,2,32,512]{3,2,1,0:T(8,128)(2,1)S(1)} %collective-permute-done.2), channel_id=1, source_target_pairs={{0,32},{32,64},{64,96},{96,128},{128,160},{160,192},{192,224},{224... | collective-permute-start | bytes 196616 | tf_op jit(solution)/shard_map/ppermute | solution.py:56
  49.9 13.4 %collective-permute-start.10 = (bf16[1,2,32,512]{3,2,1,0:T(8,128)(2,1)}, bf16[1,2,32,512]{3,2,1,0:T(8,128)(2,1)}, u32[]{:S(2)}, u32[]{:S(2)}) collective-permute-start(bf16[1,2,32,512]{3,2,1,0:T(8,128)(2,1)} %collective-permute-done.9), channel_id=1, source_target_pairs={{32,0},{64,32},{96,64},{128,96},{160,128},{192,160},{224,192},{256... | collective-permute-start | bytes 196616 | tf_op jit(solution)/shard_map/ppermute | solution.py:58
  56.6 13.4 %collective-permute-start.4 = (bf16[1,2,32,512]{3,2,1,0:T(8,128)(2,1)}, bf16[1,2,32,512]{3,2,1,0:T(8,128)(2,1)}, u32[]{:S(2)}, u32[]{:S(2)}) collective-permute-start(bf16[1,2,32,512]{3,2,1,0:T(8,128)(2,1)} %collective-permute-done.3), channel_id=1, source_target_pairs={{0,32},{32,64},{64,96},{96,128},{128,160},{160,192},{192,224},{224... | collective-permute-start | bytes 196616 | tf_op jit(solution)/shard_map/ppermute | solution.py:56
  61.4 10.6 %copy-start.16 = (s32[32]{0:T(128)S(1)}, s32[32]{0:T(128)}, u32[]{:S(2)}) copy-start(s32[32]{0:T(128)} %fusion.26) | copy-start | bytes 388
  61.4 39.6 %copy-start.14 = (bf16[1,2,32,512]{3,2,1,0:T(8,128)(2,1)S(1)}, bf16[1,2,32,512]{3,2,1,0:T(8,128)(2,1)}, u32[]{:S(2)}) copy-start(bf16[1,2,32,512]{3,2,1,0:T(8,128)(2,1)} %copy-done.13) | copy-start | bytes 196612
  61.4 40.2 %copy-start.12 = (bf16[1,2,32,512]{3,2,1,0:T(8,128)(2,1)S(1)}, bf16[1,2,32,512]{3,2,1,0:T(8,128)(2,1)}, u32[]{:S(2)}) copy-start(bf16[1,2,32,512]{3,2,1,0:T(8,128)(2,1)} %copy-done.11) | copy-start | bytes 196612
  61.4 40.8 %copy-start.10 = (bf16[1,2,32,512]{3,2,1,0:T(8,128)(2,1)S(1)}, bf16[1,2,32,512]{3,2,1,0:T(8,128)(2,1)}, u32[]{:S(2)}) copy-start(bf16[1,2,32,512]{3,2,1,0:T(8,128)(2,1)} %copy-done.9) | copy-start | bytes 196612
  61.4 41.5 %copy-start.6 = (bf16[1,2,32,512]{3,2,1,0:T(8,128)(2,1)S(1)}, bf16[1,2,32,512]{3,2,1,0:T(8,128)(2,1)}, u32[]{:S(2)}) copy-start(bf16[1,2,32,512]{3,2,1,0:T(8,128)(2,1)} %param.11) | copy-start | bytes 196612
  61.4 42.1 %copy-start.8 = (bf16[1,2,32,512]{3,2,1,0:T(8,128)(2,1)S(1)}, bf16[1,2,32,512]{3,2,1,0:T(8,128)(2,1)}, u32[]{:S(2)}) copy-start(bf16[1,2,32,512]{3,2,1,0:T(8,128)(2,1)} %copy-done.7) | copy-start | bytes 196612
  63.3 8.7 %collective-permute-start.11 = (bf16[1,2,32,512]{3,2,1,0:T(8,128)(2,1)}, bf16[1,2,32,512]{3,2,1,0:T(8,128)(2,1)S(1)}, u32[]{:S(2)}, u32[]{:S(2)}) collective-permute-start(bf16[1,2,32,512]{3,2,1,0:T(8,128)(2,1)} %collective-permute-done.10), channel_id=1, source_target_pairs={{32,0},{64,32},{96,64},{128,96},{160,128},{192,160},{224,192},{256... | collective-permute-start | bytes 196616 | tf_op jit(solution)/shard_map/ppermute | solution.py:58
  70.0 8.7 %collective-permute-start.5 = (bf16[1,2,32,512]{3,2,1,0:T(8,128)(2,1)}, bf16[1,2,32,512]{3,2,1,0:T(8,128)(2,1)S(1)}, u32[]{:S(2)}, u32[]{:S(2)}) collective-permute-start(bf16[1,2,32,512]{3,2,1,0:T(8,128)(2,1)} %collective-permute-done.4), channel_id=1, source_target_pairs={{0,32},{32,64},{64,96},{96,128},{128,160},{160,192},{192,224},{224... | collective-permute-start | bytes 196616 | tf_op jit(solution)/shard_map/ppermute | solution.py:56
  72.0 8.7 %collective-permute-start.12 = (bf16[1,2,32,512]{3,2,1,0:T(8,128)(2,1)S(1)}, bf16[1,2,32,512]{3,2,1,0:T(8,128)(2,1)S(1)}, u32[]{:S(2)}, u32[]{:S(2)}) collective-permute-start(bf16[1,2,32,512]{3,2,1,0:T(8,128)(2,1)S(1)} %collective-permute-done.11), channel_id=1, source_target_pairs={{32,0},{64,32},{96,64},{128,96},{160,128},{192,160},{224,192},{256... | collective-permute-start | bytes 196616 | tf_op jit(solution)/shard_map/ppermute | solution.py:58
  78.7 8.7 %collective-permute-start.6 = (bf16[1,2,32,512]{3,2,1,0:T(8,128)(2,1)S(1)}, bf16[1,2,32,512]{3,2,1,0:T(8,128)(2,1)S(1)}, u32[]{:S(2)}, u32[]{:S(2)}) collective-permute-start(bf16[1,2,32,512]{3,2,1,0:T(8,128)(2,1)S(1)} %collective-permute-done.5), channel_id=1, source_target_pairs={{0,32},{32,64},{64,96},{96,128},{128,160},{160,192},{192,224},{224... | collective-permute-start | bytes 196616 | tf_op jit(solution)/shard_map/ppermute | solution.py:56
  80.6 8.6 %collective-permute-start.13 = (bf16[1,2,32,512]{3,2,1,0:T(8,128)(2,1)S(1)}, bf16[1,2,32,512]{3,2,1,0:T(8,128)(2,1)S(1)}, u32[]{:S(2)}, u32[]{:S(2)}) collective-permute-start(bf16[1,2,32,512]{3,2,1,0:T(8,128)(2,1)S(1)} %collective-permute-done.12), channel_id=1, source_target_pairs={{32,0},{64,32},{96,64},{128,96},{160,128},{192,160},{224,192},{256... | collective-permute-start | bytes 196616 | tf_op jit(solution)/shard_map/ppermute | solution.py:58
  87.3 8.8 %collective-permute-start.7 = (bf16[1,2,32,512]{3,2,1,0:T(8,128)(2,1)S(1)}, bf16[1,2,32,512]{3,2,1,0:T(8,128)(2,1)S(1)}, u32[]{:S(2)}, u32[]{:S(2)}) collective-permute-start(bf16[1,2,32,512]{3,2,1,0:T(8,128)(2,1)S(1)} %collective-permute-done.6), channel_id=1, source_target_pairs={{0,32},{32,64},{64,96},{96,128},{128,160},{160,192},{192,224},{224... | collective-permute-start | bytes 196616 | tf_op jit(solution)/shard_map/ppermute | solution.py:56
  89.3 19.6 %collective-permute-start.14 = (bf16[1,2,32,512]{3,2,1,0:T(8,128)(2,1)S(1)}, bf16[1,2,32,512]{3,2,1,0:T(8,128)(2,1)S(1)}, u32[]{:S(2)}, u32[]{:S(2)}) collective-permute-start(bf16[1,2,32,512]{3,2,1,0:T(8,128)(2,1)S(1)} %collective-permute-done.13), channel_id=1, source_target_pairs={{32,0},{64,32},{96,64},{128,96},{160,128},{192,160},{224,192},{256... | collective-permute-start | bytes 196616 | tf_op jit(solution)/shard_map/ppermute | solution.py:58
  113.0 3.2 %copy-start = (bf16[1,2,512,512]{3,2,1,0:T(8,128)(2,1)S(1)}, bf16[1,2,512,512]{3,2,1,0:T(8,128)(2,1)}, u32[]{:S(2)}) copy-start(bf16[1,2,512,512]{3,2,1,0:T(8,128)(2,1)} %all-gather.2.cloned.1.call-done) | copy-start | bytes 3145732
  (6 other events, 13.1 us)
Sparse Core Ops, SparseCore 0:
  17.0 57.6 all-gather.1
